TPU v7x, 32 devices: a whole 2x2x4 slice. The times are simulated.
32 devices in a mesh: seq: 8 (over z, y), fsdp: 4 (over x, core).
Axes of the slice: x: 2, y: 2, z: 4, core: 2. Of those that a mesh axis runs over, the one named last changes fastest.
Arguments:
- tokens: bfloat16 [2048, 2048], P('seq', 'fsdp'), may hold values from -6 to 6
- deal_order: int32 [8, 8], replicated, may hold values from 0 to 7, each once within a row
- lengths: int32 [4], replicated, may hold values from 1 to 1024, 2048 in all
- x_weight: bfloat16 [2048, 1536], P(None, 'fsdp'), may hold values from -0.0390625 to 0.0390625
- z_weight: bfloat16 [2048, 1536], P(None, 'fsdp'), may hold values from -0.125 to 0.125
- shared_weight: bfloat16 [2048, 512], P('fsdp'), may hold values from -0.0390625 to 0.0390625
- step_weight: bfloat16 [2048, 24], P(None, 'fsdp'), may hold values from -0.125 to 0.125
- conv_heads: float32 [4, 1536], P(None, 'fsdp'), may hold values from -3 to 3
- conv_shared: float32 [4, 512], replicated, may hold values from -3 to 3
- step_bias: float32 [24], P('fsdp'), as said below
- decay_log: float32 [24], P('fsdp'), may hold values from -7.1 to -2.8, as said below
- skip_gain: float32 [24], P('fsdp'), may hold values from 0.5 to 1.5
Outputs:
- mixed: bfloat16 [2048, 1536], P('seq', 'fsdp')
Inputs may be any that keep to these rules, and one draw needn't show every extreme that they name: `deal_order`: each row is a permutation of 0 to 7. The lengths sum to 2048. `decay_log`: one value a head. `step_bias`: one value a head.
All inputs are finite; a program needn't handle non-finite values.
Results may differ from a plain program's by a relative error of at most 0.0095.
Values may be sent and summed in bfloat16 or wider, within the bound.
No kernel may reach another device: no remote copies, remote signals or barrier semaphores. Data moves between devices by JAX's collectives and lax.ppermute only.
A program may use at most 128 MiB of HBM per device.

v0:
```python
import jax
import jax.numpy as jnp
from jax import lax
from jax.sharding import PartitionSpec as P

precise = lax.Precision.HIGHEST


def shifted(array, axis, by):
    count = lax.axis_size(axis)
    pairs = [(i, i + by) for i in range(count) if 0 <= i + by < count]
    return lax.ppermute(array, axis, pairs)


def prefix(part, axis, combine, identity):
    place = lax.axis_index(axis)
    gathered = jax.tree.map(lambda a: lax.all_gather(a, axis), part)
    state = jax.tree.map(lambda a, e: jnp.zeros_like(a) + jnp.asarray(e, a.dtype), part, identity)

    def one(turn, state):
        return combine(
            state, jax.tree.map(lambda a: lax.dynamic_index_in_dim(a, turn, 0, False), gathered)
        )

    return lax.fori_loop(0, place, one, state)


def segment_of(positions, lengths):
    prompt_ends = jnp.cumsum(lengths)
    counted = (positions[:, None] >= prompt_ends[None, :]).astype(jnp.int32)
    return jnp.sum(counted, axis=1)


def causal_conv(extended, segment_ids, weights, conv_width):
    out_rows = extended.shape[0] - conv_width + 1
    target = segment_ids[conv_width - 1 :]
    running = jnp.zeros((out_rows, extended.shape[1]), jnp.float32)
    for tap_index in range(conv_width):
        matched = (segment_ids[tap_index : tap_index + out_rows] == target).astype(jnp.float32)
        running = (
            running
            + weights[tap_index][None, :]
            * extended[tap_index : tap_index + out_rows]
            * matched[:, None]
        )
    return running


def local_terms(x_heads, b_rows, c_rows, step_size, decay_log, segment_ids, seg_before):
    log_decay = -jnp.exp(decay_log)[None, :] * step_size
    cum_decay = jnp.cumsum(log_decay, axis=0)
    positions_in = jnp.arange(x_heads.shape[0], dtype=jnp.int32)
    same_prompt = (segment_ids[:, None] == segment_ids[None, :]) & (
        positions_in[:, None] >= positions_in[None, :]
    )
    decay_gap = cum_decay.T[:, :, None] - cum_decay.T[:, None, :]
    decay_matrix = jnp.exp(jnp.where(same_prompt[None], decay_gap, -jnp.inf))
    scores = jnp.dot(c_rows, b_rows.T, precision=precise)
    x_step = x_heads * step_size[:, :, None]
    intra = jnp.einsum("hts,shp->thp", scores[None] * decay_matrix, x_step, precision=precise)
    to_end = jnp.exp(
        jnp.where(
            (segment_ids == segment_ids[-1])[:, None], cum_decay[-1][None, :] - cum_decay, -jnp.inf
        )
    )
    state_out = jnp.einsum("shp,sn->hpn", x_step * to_end[:, :, None], b_rows, precision=precise)
    carried = segment_ids == seg_before
    carry_in = jnp.exp(jnp.where(carried[:, None], cum_decay, -jnp.inf))
    block_decay = jnp.where(carried[-1], jnp.exp(cum_decay[-1]), 0.0)
    return (intra, state_out, carry_in, block_decay)


def combine(earlier, later):
    return (earlier[0] * later[0], later[0][:, None, None] * earlier[1] + later[1])


def per_device(
    tokens,
    deal_order,
    lengths,
    x_weight,
    z_weight,
    shared_weight,
    step_weight,
    conv_heads,
    conv_shared,
    step_bias,
    decay_log,
    skip_gain,
):
    seq_count = lax.axis_size("seq")
    own_index = lax.axis_index("seq")
    tok_dev = tokens.shape[0]
    piece_rows = tok_dev // seq_count
    slot_rows = tokens.reshape(seq_count, piece_rows, tokens.shape[1])
    arrived = lax.all_to_all(slot_rows, "seq", split_axis=0, concat_axis=0, tiled=True)
    dealt_row = lax.dynamic_slice_in_dim(deal_order, own_index, 1, 0)[0]
    inverse = jnp.argsort(dealt_row)
    stream_block = jnp.take(arrived, inverse, axis=0).reshape(tok_dev, tokens.shape[1])
    inner_dev = x_weight.shape[1]
    heads_dev = step_weight.shape[1]
    head_dim = inner_dev // heads_dev
    state_dim = shared_weight.shape[1] // 2
    w_full = lax.all_gather(shared_weight, "fsdp", axis=0, tiled=True)
    weight_list = (x_weight, z_weight, step_weight, w_full)
    feature_part = lax.all_gather(stream_block, "fsdp", axis=1, tiled=True)
    x_acc, z_acc, step_acc, bc_acc = tuple(
        (
            jnp.dot(feature_part, weight, preferred_element_type=jnp.float32)
            for weight in weight_list
        )
    )
    x_raw = x_acc.astype(jnp.bfloat16)
    z_raw = z_acc.astype(jnp.bfloat16)
    bc_raw = bc_acc.astype(jnp.bfloat16)
    step_size = jax.nn.softplus(step_acc + step_bias[None, :])
    mixed_in = jnp.concatenate([x_raw, bc_raw], axis=1)
    conv_width = conv_heads.shape[0]
    prior_rows = shifted(mixed_in[tok_dev - conv_width + 1 :], "seq", 1)
    first_pos = own_index * tok_dev
    positions = first_pos - (conv_width - 1) + jnp.arange(tok_dev + conv_width - 1, dtype=jnp.int32)
    seg_ext = segment_of(positions, lengths)
    extended = jnp.concatenate([prior_rows, mixed_in], axis=0).astype(jnp.float32)
    activated = jax.nn.silu(
        causal_conv(
            extended, seg_ext, jnp.concatenate([conv_heads, conv_shared], axis=1), conv_width
        )
    )
    segment_ids = seg_ext[conv_width - 1 :]
    seg_before = jnp.where(own_index == 0, -1, seg_ext[conv_width - 2])
    x_heads = activated[:, :inner_dev].reshape(tok_dev, heads_dev, head_dim)
    b_rows = activated[:, inner_dev : inner_dev + state_dim]
    c_rows = activated[:, inner_dev + state_dim :]
    intra, state_out, carry_in, block_decay = local_terms(
        x_heads, b_rows, c_rows, step_size, decay_log, segment_ids, seg_before
    )
    identity = (jnp.ones_like(block_decay), jnp.zeros_like(state_out))
    _, state_in = prefix((block_decay, state_out), "seq", combine, identity)
    incoming = jnp.einsum("tn,hpn->thp", c_rows, state_in, precision=precise)
    y_block = intra + carry_in[:, :, None] * incoming + skip_gain[None, :, None] * x_heads
    gated = (y_block.reshape(tok_dev, inner_dev) * jax.nn.silu(z_raw.astype(jnp.float32))).astype(
        jnp.bfloat16
    )
    ordered = gated.reshape(seq_count, piece_rows, inner_dev)
    outgoing = jnp.take(ordered, dealt_row, axis=0)
    returned = lax.all_to_all(outgoing, "seq", split_axis=0, concat_axis=0, tiled=True)
    return returned.reshape(tok_dev, inner_dev)


def solution(mesh):
    return jax.shard_map(
        per_device,
        mesh=mesh,
        in_specs=(
            P("seq", "fsdp"),
            P(),
            P(),
            P(None, "fsdp"),
            P(None, "fsdp"),
            P("fsdp", None),
            P(None, "fsdp"),
            P(None, "fsdp"),
            P(),
            P("fsdp"),
            P("fsdp"),
            P("fsdp"),
        ),
        out_specs=P("seq", "fsdp"),
        check_vma=False,
    )
```

profile of v0, /device:TPU:0, one launch (start us, length us, event | category | flops | bytes accessed | tf_op | source)
XLA Modules:
  0.0 173.2 jit_solution(6664324433288918847)
XLA Ops:
  6.6 7.4 %all-to-all-start = ((bf16[8,32,512]{2,1,0:T(8,128)(2,1)}), bf16[8,32,512]{2,1,0:T(8,128)(2,1)S(1)}, u32[]{:S(2)}, u32[]{:S(2)}) async-start(bf16[8,32,512]{2,1,0:T(8,128)(2,1)} %bitcast.90), calls=%async_computation | async-start | bytes 524288 | tf_op jit(solution)/shard_map/all_to_all | solution.py:96
  14.0 1.3 compare_and_fusion.1
  15.3 1.0 sort.17
  16.3 0.1 broadcast_in_dim.88
  16.4 0.1 broadcast_in_dim.89
  16.5 6.5 %all-to-all-done = bf16[8,32,512]{2,1,0:T(8,128)(2,1)S(1)} async-done(((bf16[8,32,512]{2,1,0:T(8,128)(2,1)}), bf16[8,32,512]{2,1,0:T(8,128)(2,1)S(1)}, u32[]{:S(2)}, u32[]{:S(2)}) %all-to-all-start) | async-done | bytes 262176 | tf_op jit(solution)/shard_map/all_to_all | solution.py:96
  22.9 0.6 gather_fusion
  23.5 0.8 bitcast_select_fusion
  24.3 0.0 all-gather.8.cloned.1.call-start
  24.4 0.7 all-gather.8.cloned.1.call-update
  25.2 0.2 reduce-window.18
  25.3 0.1 convert_reduce_fusion
  25.4 0.6 fusion.51
  26.6 0.7 broadcast_compare_fusion
  27.4 0.6 slice.89
  28.0 12.2 %all-gather.6.cloned.1.call-done = bf16[256,2048]{1,0:T(8,128)(2,1)} async-done(((bf16[256,512]{1,0:T(8,128)(2,1)}), bf16[256,2048]{1,0:T(8,128)(2,1)}) %all-gather.6.cloned.1.call-update) | async-done | bytes 1048592 | tf_op jit(solution)/shard_map/all_gather | solution.py:106
  40.3 1.6 fusion.41
  41.9 1.8 %reduce-window.19 = f32[6,2,128]{2,1,0:T(2,128)S(1)} reduce-window(f32[6,2,128]{2,1,0:T(2,128)S(1)} %reshape.175, f32[]{:T(128)} %constant.76.clone.1), window={size=1x1x128 pad=0_0x0_0x127_0}, to_apply=%region_3.4 | reduce-window | flops 195072 | bytes 12292 | tf_op jit(solution)/shard_map/reduce-window.1
  43.8 0.1 slice.107
  43.8 0.1 copy.47
  44.0 0.1 copy.48
  44.1 0.1 add_bitcast_fusion
  44.2 0.8 slice_reduce_fusion
  45.0 0.1 select_exponential_fusion.1
  45.1 1.9 %convolution_convert_fusion.2 = bf16[256,384]{1,0:T(8,128)(2,1)S(1)} fusion(bf16[256,2048]{1,0:T(8,128)(2,1)} %all-gather.6.cloned.1.call-done, bf16[2048,384]{1,0:T(8,128)(2,1)S(1)} %copy-done), kind=kOutput, calls=%fused_computation.16 | convolution fusion | flops 402751488 | bytes 2818048 | tf_op jit(solution)/shard_map/dot_general | solution.py:109
  47.0 17.4 %all-gather.8.cloned.1.call-done = bf16[2048,512]{1,0:T(8,128)(2,1)} async-done(((bf16[512,512]{1,0:T(8,128)(2,1)}), bf16[2048,512]{1,0:T(8,128)(2,1)}) %all-gather.8.cloned.1.call-update) | async-done | bytes 2097168 | tf_op jit(solution)/shard_map/all_gather | solution.py:104
  64.5 2.3 %convolution_convert_fusion = bf16[256,512]{1,0:T(8,128)(2,1)S(1)} fusion(bf16[256,2048]{1,0:T(8,128)(2,1)S(1)} %copy-done.1, bf16[2048,512]{1,0:T(8,128)(2,1)} %all-gather.8.cloned.1.call-done), kind=kOutput, calls=%fused_computation.12 | convolution fusion | flops 537001984 | bytes 3407872 | tf_op jit(solution)/shard_map/dot_general | solution.py:109
  66.8 3.4 %collective-permute-start = (bf16[3,896]{1,0:T(4,128)(2,1)S(1)}, bf16[3,896]{1,0:T(4,128)(2,1)S(1)}, u32[]{:S(2)}, u32[]{:S(2)}) collective-permute-start(bf16[3,896]{1,0:T(4,128)(2,1)S(1)} %pad_maximum_fusion), channel_id=1, source_target_pairs={{0,4},{4,8},{8,12},{12,16},{16,20},{20,24},{24,28},{1,5},{5,9},{9,... | collective-permute-start | bytes 16136 | tf_op jit(solution)/shard_map/ppermute | solution.py:12
  70.2 1.3 collective-permute-done
  71.5 0.1 maximum_convert_fusion
  71.6 0.7 divide_multiply_fusion
  72.3 0.2 copy.46
  72.5 1.2 fusion.26
  73.8 0.1 slice.74
  73.8 0.7 fusion.47
  74.5 0.6 pad_clamp_fusion
  75.1 0.7 fusion.32
  75.9 21.6 %all-gather.1 = f32[8,1,6]{2,1,0:T(1,128)} all-gather(f32[1,1,6]{2,1,0:T(1,128)S(1)} %bitcast.96), channel_id=1, replica_groups=mesh['seq'=8,'fsdp'=4] {'seq'}, dimensions={0}, use_global_device_ids=true | all-gather | bytes 216 | tf_op jit(solution)/shard_map/all_gather | solution.py:17
  97.5 0.4 fusion.34
  97.9 37.2 %all-gather.10.cloned.1.call-done = f32[48,64,256]{2,1,0:T(8,128)} async-done(((f32[6,64,256]{2,1,0:T(8,128)}), f32[48,64,256]{2,1,0:T(8,128)}) %all-gather.10.cloned.1.call-update) | async-done | bytes 3145744 | tf_op jit(solution)/shard_map/all_gather | solution.py:17
  135.2 0.5 convolution_multiply_fusion
  135.7 2.8 %fusion.11 = f32[256,6,64]{0,2,1:T(8,128)S(1)} fusion(f32[256,6,64]{0,2,1:T(8,128)S(1)} %convolution_multiply_fusion, f32[6,256]{1,0:T(8,128)} %bitcast.93, f32[256,256]{1,0:T(8,128)S(1)} %fusion.34, pred[256,256]{1,0:T(8,128)(4,1)} %fusion.32, f32[256,6,64]{0,2,1:T(8,128)S(1)} %bitcast.86, f32[6]{0:T(128)} %param.25, f32[256,6]{0,1:T(8,128)S(1)} %compare_select_fusion.1), kind=kOutput, calls=%fused_computation.11 | convolution fusion | flops 303562752 | bytes 1519640 | tf_op jit(solution)/shard_map/hts,shp->thp/dot_general | solution.py:60
  138.5 0.2 copy.49
  138.7 2.5 %multiply_convert_fusion = bf16[256,384]{1,0:T(8,128)(2,1)S(1)} fusion(f32[256,384]{1,0:T(8,128)S(1)} %copy.49, bf16[256,2048]{1,0:T(8,128)(2,1)} %all-gather.6.cloned.1.call-done, bf16[2048,384]{1,0:T(8,128)(2,1)} %param.18), kind=kOutput, calls=%fused_computation.35 | convolution fusion | flops 403439616 | bytes 3211264 | tf_op jit(solution)/shard_map/dot_general | solution.py:109
  141.2 0.7 gather_fusion.1
  141.9 0.1 broadcast_select_fusion
  142.0 24.0 %all_to_all.10 = bf16[8,32,384]{2,1,0:T(8,128)(2,1)S(1)} all-to-all(bf16[8,32,384]{2,1,0:T(8,128)(2,1)S(1)} %broadcast_select_fusion), channel_id=1, replica_groups=mesh['seq'=8,'fsdp'=4] {'seq'}, dimensions={0} | all-to-all | bytes 393216 | tf_op jit(solution)/shard_map/all_to_all | solution.py:146
  166.0 0.7 copy.67
  (42 shorter events, 0.4 us)
Async XLA Ops:
  6.5 38.6 %copy-start = (bf16[2048,384]{1,0:T(8,128)(2,1)S(1)}, bf16[2048,384]{1,0:T(8,128)(2,1)}, u32[]{:S(2)}) copy-start(bf16[2048,384]{1,0:T(8,128)(2,1)} %param.17) | copy-start | bytes 4718596
  6.5 18.6 %copy-start.8 = (s32[4]{0:T(128)S(1)}, s32[4]{0:T(128)}, u32[]{:S(2)}) copy-start(s32[4]{0:T(128)} %param.16) | copy-start | bytes 52
  6.5 21.4 %copy-start.5 = (f32[4,384]{1,0:T(4,128)S(1)}, f32[4,384]{1,0:T(4,128)}, u32[]{:S(2)}) copy-start(f32[4,384]{1,0:T(4,128)} %param.21) | copy-start | bytes 18436
  6.5 21.4 %copy-start.4 = (f32[4,512]{1,0:T(4,128)S(1)}, f32[4,512]{1,0:T(4,128)}, u32[]{:S(2)}) copy-start(f32[4,512]{1,0:T(4,128)} %param.22) | copy-start | bytes 24580
  6.5 21.5 %copy-start.9 = (f32[6]{0:T(128)S(1)}, f32[6]{0:T(128)}, u32[]{:S(2)}) copy-start(f32[6]{0:T(128)} %param.24) | copy-start | bytes 76
  6.5 33.7 %copy-start.2 = (bf16[2048,6]{0,1:T(8,128)(2,1)S(1)}, bf16[2048,6]{0,1:T(8,128)(2,1)}, u32[]{:S(2)}) copy-start(bf16[2048,6]{0,1:T(8,128)(2,1)} %param.20) | copy-start | bytes 73732
  6.6 33.7 %copy-start.7 = (f32[6]{0:T(128)S(1)}, f32[6]{0:T(128)}, u32[]{:S(2)}) copy-start(f32[6]{0:T(128)} %param.23) | copy-start | bytes 76
  6.6 16.3 %all-to-all-start = ((bf16[8,32,512]{2,1,0:T(8,128)(2,1)}), bf16[8,32,512]{2,1,0:T(8,128)(2,1)S(1)}, u32[]{:S(2)}, u32[]{:S(2)}) async-start(bf16[8,32,512]{2,1,0:T(8,128)(2,1)} %bitcast.90), calls=%async_computation | async-start | bytes 524288 | tf_op jit(solution)/shard_map/all_to_all | solution.py:96
  14.0 26.3 %all-gather.6.cloned.1.call-start = ((), (), s32[]{:S(2)}) async-start(), calls=%async_computation.2 | async-start | bytes 1310720 | tf_op jit(solution)/shard_map/all_gather | solution.py:106
  24.3 40.1 %all-gather.8.cloned.1.call-start = ((), (), s32[]{:S(2)}) async-start(), calls=%async_computation.3 | async-start | bytes 2621440 | tf_op jit(solution)/shard_map/all_gather | solution.py:104
  25.1 110.1 %all-gather.10.cloned.1.call-start = ((), (), s32[]{:S(2)}) async-start(), calls=%async_computation.4 | async-start | bytes 3538944 | tf_op jit(solution)/shard_map/all_gather | solution.py:17
  41.9 22.5 %copy-start.1 = (bf16[256,2048]{1,0:T(8,128)(2,1)S(1)}, bf16[256,2048]{1,0:T(8,128)(2,1)}, u32[]{:S(2)}) copy-start(bf16[256,2048]{1,0:T(8,128)(2,1)} %all-gather.6.cloned.1.call-done) | copy-start | bytes 3145732
  44.2 0.8 copy-start.3
  66.8 4.7 %collective-permute-start = (bf16[3,896]{1,0:T(4,128)(2,1)S(1)}, bf16[3,896]{1,0:T(4,128)(2,1)S(1)}, u32[]{:S(2)}, u32[]{:S(2)}) collective-permute-start(bf16[3,896]{1,0:T(4,128)(2,1)S(1)} %pad_maximum_fusion), channel_id=1, source_target_pairs={{0,4},{4,8},{8,12},{12,16},{16,20},{20,24},{24,28},{1,5},{5,9},{9,... | collective-permute-start | bytes 16136 | tf_op jit(solution)/shard_map/ppermute | solution.py:12
  138.7 3.2 %copy-start.6 = (pred[8]{0:T(512)(128)(4,1)S(1)}, pred[8]{0:T(512)(128)(4,1)}, u32[]{:S(2)}) copy-start(pred[8]{0:T(512)(128)(4,1)} %get-tuple-element.68) | copy-start | bytes 28
Sparse Core Ops, SparseCore 0:
  24.5 15.7 all-gather.5
  41.8 22.5 all-gather.7
  73.9 61.2 all-gather.9
where the time goes:
time: 174 us; the launch traced here: 173 us
  waiting for transfers between devices  75.4 us (43%)
  blocking collectives  45.7 us (26%)
  between operations  14 us (8%)
  matrix products  13.3 us (8%)
  starting transfers between devices  10.9 us (6%)
  other arithmetic  9.84 us (6%)
  local copies, waits for them, and re-layouts  4.14 us (2%)
    all_gather x1, waiting for transfers between devices, prefix(): gathered = jax.tree.map(lambda a: lax.all_gather(a, axis), part)  37.2 us
    all_to_all x1, blocking collectives, per_device(): lax.all_to_all(outgoing, 'seq', split_axis=0, concat_axis=0, tiled=True)  24 us
    all_gather x1, blocking collectives, prefix(): gathered = jax.tree.map(lambda a: lax.all_gather(a, axis), part)  21.6 us
    all_gather x1, waiting for transfers between devices, per_device(): w_full = lax.all_gather(shared_weight, 'fsdp', axis=0, tiled=True)  17.4 us
    all_gather x1, waiting for transfers between devices, per_device(): feature_part = lax.all_gather(stream_block, 'fsdp', axis=1, tiled=True)  12.2 us
    dot_general x4, matrix products, per_device(): jnp.dot(feature_part, weight, preferred_element_type=jnp.float32)  8.34 us
    all_to_all x1, starting transfers between devices, per_device(): lax.all_to_all(slot_rows, 'seq', split_axis=0, concat_axis=0, tiled=True)  7.42 us
    all_to_all x1, waiting for transfers between devices, per_device(): lax.all_to_all(slot_rows, 'seq', split_axis=0, concat_axis=0, tiled=True)  6.45 us
  transfers between devices with their start and end apart: 5, of which 5 were waited for; matrix products, arithmetic and copies ran while one was open for 8% of the time, Pallas kernels for 0%

commit v1 on v0

--- a/solution.py
+++ b/solution.py
@@ -4,6 +4,18 @@
 from jax.sharding import PartitionSpec as P
 
 precise = lax.Precision.HIGHEST
+
+
+def cut_along(x, dim, size):
+    shape = x.shape
+    pieces = x.reshape(*shape[:dim], size, shape[dim] // size, *shape[dim + 1 :])
+    return jnp.moveaxis(pieces, dim, 0)
+
+
+def in_order(blocks, dim):
+    blocks = jnp.moveaxis(blocks, 0, dim)
+    dims = blocks.shape
+    return blocks.reshape(*dims[:dim], dims[dim] * dims[dim + 1], *dims[dim + 2 :])
 
 
 def shifted(array, axis, by):
@@ -143,7 +155,14 @@
     )
     ordered = gated.reshape(seq_count, piece_rows, inner_dev)
     outgoing = jnp.take(ordered, dealt_row, axis=0)
-    returned = lax.all_to_all(outgoing, "seq", split_axis=0, concat_axis=0, tiled=True)
+    devices, index = (lax.axis_size("seq"), lax.axis_index("seq"))
+    blocks = cut_along(outgoing, 0, devices)
+    gathered_2 = [blocks[index]]
+    for step in range(1, devices):
+        sent = blocks[index ^ step]
+        gathered_2.append(lax.ppermute(sent, "seq", [(i_2, i_2 ^ step) for i_2 in range(devices)]))
+    blocks = jnp.stack(gathered_2)[index ^ jnp.arange(devices)]
+    returned = in_order(blocks, 0)
     return returned.reshape(tok_dev, inner_dev)
 
 

time: 174 us -> 179 us (1.029)
  blocking collectives: 45.7 us -> 21.8 us
  starting transfers between devices: 10.9 us -> 32.3 us
  waiting for transfers between devices: 75.4 us -> 81.1 us
    all_to_all x1 -> x0, blocking collectives: 24 us -> none  [per_device(): lax.all_to_all(outgoing, 'seq', split_axis=0, concat_axis=0, tiled=True)]
    ppermute x0 -> x7, starting transfers between devices: none -> 21.4 us  [per_device(): lax.ppermute(sent, 'seq', [(i_2, i_2 ^ step) for i_2 in range(devices)])]
    ppermute x0 -> x7, waiting for transfers between devices: none -> 6.43 us  [per_device(): lax.ppermute(sent, 'seq', [(i_2, i_2 ^ step) for i_2 in range(devices)])]
  transfers between devices with their start and end apart: 5 -> 12, of which waited for: 5 -> 8; matrix products, arithmetic and copies ran while one was open for 8% -> 8% of each run, Pallas kernels for 0% -> 0%
where the time goes in v1:
time: 179 us; the launch traced here: 178 us
  waiting for transfers between devices  81.1 us (45%)
  starting transfers between devices  32.3 us (18%)
  blocking collectives  21.8 us (12%)
  between operations  14 us (8%)
  matrix products  13.3 us (7%)
  other arithmetic  10.4 us (6%)
  local copies, waits for them, and re-layouts  4.97 us (3%)
    all_gather x1, waiting for transfers between devices, prefix(): gathered = jax.tree.map(lambda a: lax.all_gather(a, axis), part)  36.5 us
    all_gather x1, blocking collectives, prefix(): gathered = jax.tree.map(lambda a: lax.all_gather(a, axis), part)  21.8 us
    ppermute x7, starting transfers between devices, per_device(): lax.ppermute(sent, 'seq', [(i_2, i_2 ^ step) for i_2 in range(devices)])  21.4 us
    all_gather x1, waiting for transfers between devices, per_device(): w_full = lax.all_gather(shared_weight, 'fsdp', axis=0, tiled=True)  17.4 us
    all_gather x1, waiting for transfers between devices, per_device(): feature_part = lax.all_gather(stream_block, 'fsdp', axis=1, tiled=True)  12.2 us
    dot_general x4, matrix products, per_device(): jnp.dot(feature_part, weight, preferred_element_type=jnp.float32)  8.34 us
    all_to_all x1, starting transfers between devices, per_device(): lax.all_to_all(slot_rows, 'seq', split_axis=0, concat_axis=0, tiled=True)  7.42 us
    all_to_all x1, waiting for transfers between devices, per_device(): lax.all_to_all(slot_rows, 'seq', split_axis=0, concat_axis=0, tiled=True)  6.49 us
  transfers between devices with their start and end apart: 12, of which 8 were waited for; matrix products, arithmetic and copies ran while one was open for 8% of the time, Pallas kernels for 0%

profile of v1, /device:TPU:0, one launch (start us, length us, event | category | flops | bytes accessed | tf_op | source)
XLA Modules:
  0.0 177.9 jit_solution(2266336260900227268)
XLA Ops:
  6.6 7.4 %all-to-all-start = ((bf16[8,32,512]{2,1,0:T(8,128)(2,1)}), bf16[8,32,512]{2,1,0:T(8,128)(2,1)S(1)}, u32[]{:S(2)}, u32[]{:S(2)}) async-start(bf16[8,32,512]{2,1,0:T(8,128)(2,1)} %bitcast.108), calls=%async_computation | async-start | bytes 524288 | tf_op jit(solution)/shard_map/all_to_all | solution.py:108
  14.0 1.2 compare_and_fusion.1
  15.3 1.0 sort.17
  16.4 6.5 %all-to-all-done = bf16[8,32,512]{2,1,0:T(8,128)(2,1)S(1)} async-done(((bf16[8,32,512]{2,1,0:T(8,128)(2,1)}), bf16[8,32,512]{2,1,0:T(8,128)(2,1)S(1)}, u32[]{:S(2)}, u32[]{:S(2)}) %all-to-all-start) | async-done | bytes 262176 | tf_op jit(solution)/shard_map/all_to_all | solution.py:108
  22.9 0.6 gather_fusion
  23.5 0.8 bitcast_select_fusion
  24.4 0.7 all-gather.8.cloned.1.call-update
  25.2 0.2 reduce-window.18
  25.4 0.6 fusion.52
  26.7 0.7 broadcast_compare_fusion
  27.4 0.6 slice.89
  28.1 12.2 %all-gather.6.cloned.1.call-done = bf16[256,2048]{1,0:T(8,128)(2,1)} async-done(((bf16[256,512]{1,0:T(8,128)(2,1)}), bf16[256,2048]{1,0:T(8,128)(2,1)}) %all-gather.6.cloned.1.call-update) | async-done | bytes 1048592 | tf_op jit(solution)/shard_map/all_gather | solution.py:118
  40.3 1.6 fusion.41
  42.0 1.8 %reduce-window.19 = f32[6,2,128]{2,1,0:T(2,128)S(1)} reduce-window(f32[6,2,128]{2,1,0:T(2,128)S(1)} %reshape.204, f32[]{:T(128)} %constant.84.clone.1), window={size=1x1x128 pad=0_0x0_0x127_0}, to_apply=%region_3.4 | reduce-window | flops 195072 | bytes 12292 | tf_op jit(solution)/shard_map/reduce-window.1
  43.9 0.1 copy.47
  44.0 0.1 copy.48
  44.2 0.8 slice_reduce_fusion
  45.1 1.9 %convolution_convert_fusion.2 = bf16[256,384]{1,0:T(8,128)(2,1)S(1)} fusion(bf16[256,2048]{1,0:T(8,128)(2,1)} %all-gather.6.cloned.1.call-done, bf16[2048,384]{1,0:T(8,128)(2,1)S(1)} %copy-done), kind=kOutput, calls=%fused_computation.17 | convolution fusion | flops 402751488 | bytes 2818048 | tf_op jit(solution)/shard_map/dot_general | solution.py:121
  47.1 17.4 %all-gather.8.cloned.1.call-done = bf16[2048,512]{1,0:T(8,128)(2,1)} async-done(((bf16[512,512]{1,0:T(8,128)(2,1)}), bf16[2048,512]{1,0:T(8,128)(2,1)}) %all-gather.8.cloned.1.call-update) | async-done | bytes 2097168 | tf_op jit(solution)/shard_map/all_gather | solution.py:116
  64.5 2.3 %convolution_convert_fusion = bf16[256,512]{1,0:T(8,128)(2,1)S(1)} fusion(bf16[256,2048]{1,0:T(8,128)(2,1)S(1)} %copy-done.1, bf16[2048,512]{1,0:T(8,128)(2,1)} %all-gather.8.cloned.1.call-done), kind=kOutput, calls=%fused_computation.13 | convolution fusion | flops 537001984 | bytes 3407872 | tf_op jit(solution)/shard_map/dot_general | solution.py:121
  66.8 3.4 %collective-permute-start = (bf16[3,896]{1,0:T(4,128)(2,1)S(1)}, bf16[3,896]{1,0:T(4,128)(2,1)S(1)}, u32[]{:S(2)}, u32[]{:S(2)}) collective-permute-start(bf16[3,896]{1,0:T(4,128)(2,1)S(1)} %pad_maximum_fusion), channel_id=1, source_target_pairs={{0,4},{4,8},{8,12},{12,16},{16,20},{20,24},{24,28},{1,5},{5,9},{9,... | collective-permute-start | bytes 16136 | tf_op jit(solution)/shard_map/ppermute | solution.py:24
  70.2 1.3 collective-permute-done
  71.5 0.1 maximum_convert_fusion
  71.6 0.7 divide_multiply_fusion
  72.3 0.2 copy.46
  72.5 1.2 fusion.26
  73.9 0.7 fusion.47
  74.6 0.6 pad_clamp_fusion.1
  75.1 0.6 pad_clamp_fusion
  75.7 0.7 fusion.32
  76.5 21.8 %all-gather.1 = f32[8,1,6]{2,1,0:T(1,128)} all-gather(f32[1,1,6]{2,1,0:T(1,128)S(1)} %bitcast.115), channel_id=1, replica_groups=mesh['seq'=8,'fsdp'=4] {'seq'}, dimensions={0}, use_global_device_ids=true | all-gather | bytes 216 | tf_op jit(solution)/shard_map/all_gather | solution.py:29
  98.3 0.4 fusion.34
  98.7 36.5 %all-gather.10.cloned.1.call-done = f32[48,64,256]{2,1,0:T(8,128)} async-done(((f32[6,64,256]{2,1,0:T(8,128)}), f32[48,64,256]{2,1,0:T(8,128)}) %all-gather.10.cloned.1.call-update) | async-done | bytes 3145744 | tf_op jit(solution)/shard_map/all_gather | solution.py:29
  135.2 0.5 convolution_multiply_fusion
  135.7 2.8 %fusion.11 = f32[256,6,64]{0,2,1:T(8,128)S(1)} fusion(f32[256,6,64]{0,2,1:T(8,128)S(1)} %convolution_multiply_fusion, f32[6,256]{1,0:T(8,128)} %bitcast.112, f32[256,256]{1,0:T(8,128)S(1)} %fusion.34, pred[256,256]{1,0:T(8,128)(4,1)} %fusion.32, f32[256,6,64]{0,2,1:T(8,128)S(1)} %bitcast.105, f32[6]{0:T(128)} %param.25, f32[256,6]{0,1:T(8,128)S(1)} %compare_select_fusion.1), kind=kOutput, calls=%fused_computation.12 | convolution fusion | flops 303562752 | bytes 1519640 | tf_op jit(solution)/shard_map/hts,shp->thp/dot_general | solution.py:72
  138.5 0.2 copy.49
  138.7 2.5 %multiply_convert_fusion = bf16[256,384]{1,0:T(8,128)(2,1)S(1)} fusion(f32[256,384]{1,0:T(8,128)S(1)} %copy.49, bf16[256,2048]{1,0:T(8,128)(2,1)} %all-gather.6.cloned.1.call-done, bf16[2048,384]{1,0:T(8,128)(2,1)} %param.18), kind=kOutput, calls=%fused_computation.36 | convolution fusion | flops 403439616 | bytes 3211264 | tf_op jit(solution)/shard_map/dot_general | solution.py:121
  141.2 0.7 gather_fusion.1
  141.9 0.1 broadcast_select_fusion
  142.0 2.5 %collective-permute-start.1 = (bf16[1,32,384]{2,1,0:T(8,128)(2,1)S(1)}, bf16[1,32,384]{2,1,0:T(8,128)(2,1)S(1)}, u32[]{:S(2)}, u32[]{:S(2)}) collective-permute-start(bf16[1,32,384]{2,1,0:T(8,128)(2,1)S(1)} %get-tuple-element.76), channel_id=1, source_target_pairs={{0,4},{4,0},{8,12},{12,8},{16,20},{20,16},{24,28},{28,24},{1,5},{5... | collective-permute-start | bytes 73736 | tf_op jit(solution)/shard_map/ppermute | solution.py:163
  144.5 5.1 %collective-permute-start.2 = (bf16[1,32,384]{2,1,0:T(8,128)(2,1)S(1)}, bf16[1,32,384]{2,1,0:T(8,128)(2,1)S(1)}, u32[]{:S(2)}, u32[]{:S(2)}) collective-permute-start(bf16[1,32,384]{2,1,0:T(8,128)(2,1)S(1)} %get-tuple-element.75), channel_id=1, source_target_pairs={{0,8},{4,12},{8,0},{12,4},{16,24},{20,28},{24,16},{28,20},{1,9},{5... | collective-permute-start | bytes 73736 | tf_op jit(solution)/shard_map/ppermute | solution.py:163
  149.6 8.5 %collective-permute-start.4 = (bf16[1,32,384]{2,1,0:T(8,128)(2,1)S(1)}, bf16[1,32,384]{2,1,0:T(8,128)(2,1)S(1)}, u32[]{:S(2)}, u32[]{:S(2)}) collective-permute-start(bf16[1,32,384]{2,1,0:T(8,128)(2,1)S(1)} %get-tuple-element.73), channel_id=1, source_target_pairs={{0,16},{4,20},{8,24},{12,28},{16,0},{20,4},{24,8},{28,12},{1,17},{... | collective-permute-start | bytes 73736 | tf_op jit(solution)/shard_map/ppermute | solution.py:163
  158.1 0.9 collective-permute-start.5
  159.0 4.4 %collective-permute-start.6 = (bf16[1,32,384]{2,1,0:T(8,128)(2,1)S(1)}, bf16[1,32,384]{2,1,0:T(8,128)(2,1)S(1)}, u32[]{:S(2)}, u32[]{:S(2)}) collective-permute-start(bf16[1,32,384]{2,1,0:T(8,128)(2,1)S(1)} %get-tuple-element.71), channel_id=1, source_target_pairs={{0,24},{4,28},{8,16},{12,20},{16,8},{20,12},{24,0},{28,4},{1,25},{... | collective-permute-start | bytes 73736 | tf_op jit(solution)/shard_map/ppermute | solution.py:163
  163.5 0.2 collective-permute-done.5
  163.7 1.7 collective-permute-done.6
  165.5 4.5 %collective-permute-done.7 = bf16[1,32,384]{2,1,0:T(8,128)(2,1)S(1)} collective-permute-done((bf16[1,32,384]{2,1,0:T(8,128)(2,1)S(1)}, bf16[1,32,384]{2,1,0:T(8,128)(2,1)S(1)}, u32[]{:S(2)}, u32[]{:S(2)}) %collective-permute-start.7) | collective-permute-done | bytes 24608 | tf_op jit(solution)/shard_map/ppermute | solution.py:163
  170.0 1.4 gather_fusion.2
  (66 shorter events, 1.2 us)
Async XLA Ops:
  6.5 38.6 %copy-start = (bf16[2048,384]{1,0:T(8,128)(2,1)S(1)}, bf16[2048,384]{1,0:T(8,128)(2,1)}, u32[]{:S(2)}) copy-start(bf16[2048,384]{1,0:T(8,128)(2,1)} %param.17) | copy-start | bytes 4718596
  6.5 18.6 %copy-start.8 = (s32[4]{0:T(128)S(1)}, s32[4]{0:T(128)}, u32[]{:S(2)}) copy-start(s32[4]{0:T(128)} %param.16) | copy-start | bytes 52
  6.5 21.4 %copy-start.5 = (f32[4,384]{1,0:T(4,128)S(1)}, f32[4,384]{1,0:T(4,128)}, u32[]{:S(2)}) copy-start(f32[4,384]{1,0:T(4,128)} %param.21) | copy-start | bytes 18436
  6.5 21.4 %copy-start.4 = (f32[4,512]{1,0:T(4,128)S(1)}, f32[4,512]{1,0:T(4,128)}, u32[]{:S(2)}) copy-start(f32[4,512]{1,0:T(4,128)} %param.22) | copy-start | bytes 24580
  6.5 21.5 %copy-start.9 = (f32[6]{0:T(128)S(1)}, f32[6]{0:T(128)}, u32[]{:S(2)}) copy-start(f32[6]{0:T(128)} %param.24) | copy-start | bytes 76
  6.5 33.7 %copy-start.2 = (bf16[2048,6]{0,1:T(8,128)(2,1)S(1)}, bf16[2048,6]{0,1:T(8,128)(2,1)}, u32[]{:S(2)}) copy-start(bf16[2048,6]{0,1:T(8,128)(2,1)} %param.20) | copy-start | bytes 73732
  6.6 33.7 %copy-start.7 = (f32[6]{0:T(128)S(1)}, f32[6]{0:T(128)}, u32[]{:S(2)}) copy-start(f32[6]{0:T(128)} %param.23) | copy-start | bytes 76
  6.6 16.3 %all-to-all-start = ((bf16[8,32,512]{2,1,0:T(8,128)(2,1)}), bf16[8,32,512]{2,1,0:T(8,128)(2,1)S(1)}, u32[]{:S(2)}, u32[]{:S(2)}) async-start(bf16[8,32,512]{2,1,0:T(8,128)(2,1)} %bitcast.108), calls=%async_computation | async-start | bytes 524288 | tf_op jit(solution)/shard_map/all_to_all | solution.py:108
  14.0 26.3 %all-gather.6.cloned.1.call-start = ((), (), s32[]{:S(2)}) async-start(), calls=%async_computation.1 | async-start | bytes 1310720 | tf_op jit(solution)/shard_map/all_gather | solution.py:118
  24.4 40.1 %all-gather.8.cloned.1.call-start = ((), (), s32[]{:S(2)}) async-start(), calls=%async_computation.2 | async-start | bytes 2621440 | tf_op jit(solution)/shard_map/all_gather | solution.py:116
  25.1 110.1 %all-gather.10.cloned.1.call-start = ((), (), s32[]{:S(2)}) async-start(), calls=%async_computation.3 | async-start | bytes 3538944 | tf_op jit(solution)/shard_map/all_gather | solution.py:29
  41.9 22.5 %copy-start.1 = (bf16[256,2048]{1,0:T(8,128)(2,1)S(1)}, bf16[256,2048]{1,0:T(8,128)(2,1)}, u32[]{:S(2)}) copy-start(bf16[256,2048]{1,0:T(8,128)(2,1)} %all-gather.6.cloned.1.call-done) | copy-start | bytes 3145732
  44.2 0.8 copy-start.3
  66.8 4.7 %collective-permute-start = (bf16[3,896]{1,0:T(4,128)(2,1)S(1)}, bf16[3,896]{1,0:T(4,128)(2,1)S(1)}, u32[]{:S(2)}, u32[]{:S(2)}) collective-permute-start(bf16[3,896]{1,0:T(4,128)(2,1)S(1)} %pad_maximum_fusion), channel_id=1, source_target_pairs={{0,4},{4,8},{8,12},{12,16},{16,20},{20,24},{24,28},{1,5},{5,9},{9,... | collective-permute-start | bytes 16136 | tf_op jit(solution)/shard_map/ppermute | solution.py:24
  138.7 3.2 %copy-start.6 = (pred[8]{0:T(512)(128)(4,1)S(1)}, pred[8]{0:T(512)(128)(4,1)}, u32[]{:S(2)}) copy-start(pred[8]{0:T(512)(128)(4,1)} %get-tuple-element.68) | copy-start | bytes 28
  142.0 17.0 %collective-permute-start.1 = (bf16[1,32,384]{2,1,0:T(8,128)(2,1)S(1)}, bf16[1,32,384]{2,1,0:T(8,128)(2,1)S(1)}, u32[]{:S(2)}, u32[]{:S(2)}) collective-permute-start(bf16[1,32,384]{2,1,0:T(8,128)(2,1)S(1)} %get-tuple-element.76), channel_id=1, source_target_pairs={{0,4},{4,0},{8,12},{12,8},{16,20},{20,16},{24,28},{28,24},{1,5},{5... | collective-permute-start | bytes 73736 | tf_op jit(solution)/shard_map/ppermute | solution.py:163
  144.5 18.9 %collective-permute-start.2 = (bf16[1,32,384]{2,1,0:T(8,128)(2,1)S(1)}, bf16[1,32,384]{2,1,0:T(8,128)(2,1)S(1)}, u32[]{:S(2)}, u32[]{:S(2)}) collective-permute-start(bf16[1,32,384]{2,1,0:T(8,128)(2,1)S(1)} %get-tuple-element.75), channel_id=1, source_target_pairs={{0,8},{4,12},{8,0},{12,4},{16,24},{20,28},{24,16},{28,20},{1,9},{5... | collective-permute-start | bytes 73736 | tf_op jit(solution)/shard_map/ppermute | solution.py:163
  149.6 13.9 %collective-permute-start.3 = (bf16[1,32,384]{2,1,0:T(8,128)(2,1)S(1)}, bf16[1,32,384]{2,1,0:T(8,128)(2,1)S(1)}, u32[]{:S(2)}, u32[]{:S(2)}) collective-permute-start(bf16[1,32,384]{2,1,0:T(8,128)(2,1)S(1)} %get-tuple-element.74), channel_id=1, source_target_pairs={{0,12},{4,8},{8,4},{12,0},{16,28},{20,24},{24,20},{28,16},{1,13},{... | collective-permute-start | bytes 73736 | tf_op jit(solution)/shard_map/ppermute | solution.py:163
  149.6 13.9 %collective-permute-start.4 = (bf16[1,32,384]{2,1,0:T(8,128)(2,1)S(1)}, bf16[1,32,384]{2,1,0:T(8,128)(2,1)S(1)}, u32[]{:S(2)}, u32[]{:S(2)}) collective-permute-start(bf16[1,32,384]{2,1,0:T(8,128)(2,1)S(1)} %get-tuple-element.73), channel_id=1, source_target_pairs={{0,16},{4,20},{8,24},{12,28},{16,0},{20,4},{24,8},{28,12},{1,17},{... | collective-permute-start | bytes 73736 | tf_op jit(solution)/shard_map/ppermute | solution.py:163
  158.1 5.6 %collective-permute-start.5 = (bf16[1,32,384]{2,1,0:T(8,128)(2,1)S(1)}, bf16[1,32,384]{2,1,0:T(8,128)(2,1)S(1)}, u32[]{:S(2)}, u32[]{:S(2)}) collective-permute-start(bf16[1,32,384]{2,1,0:T(8,128)(2,1)S(1)} %get-tuple-element.72), channel_id=1, source_target_pairs={{0,20},{4,16},{8,28},{12,24},{16,4},{20,0},{24,12},{28,8},{1,21},{... | collective-permute-start | bytes 73736 | tf_op jit(solution)/shard_map/ppermute | solution.py:163
  159.0 6.4 %collective-permute-start.6 = (bf16[1,32,384]{2,1,0:T(8,128)(2,1)S(1)}, bf16[1,32,384]{2,1,0:T(8,128)(2,1)S(1)}, u32[]{:S(2)}, u32[]{:S(2)}) collective-permute-start(bf16[1,32,384]{2,1,0:T(8,128)(2,1)S(1)} %get-tuple-element.71), channel_id=1, source_target_pairs={{0,24},{4,28},{8,16},{12,20},{16,8},{20,12},{24,0},{28,4},{1,25},{... | collective-permute-start | bytes 73736 | tf_op jit(solution)/shard_map/ppermute | solution.py:163
  163.4 6.6 %collective-permute-start.7 = (bf16[1,32,384]{2,1,0:T(8,128)(2,1)S(1)}, bf16[1,32,384]{2,1,0:T(8,128)(2,1)S(1)}, u32[]{:S(2)}, u32[]{:S(2)}) collective-permute-start(bf16[1,32,384]{2,1,0:T(8,128)(2,1)S(1)} %get-tuple-element.70), channel_id=1, source_target_pairs={{0,28},{4,24},{8,20},{12,16},{16,12},{20,8},{24,4},{28,0},{1,29},{... | collective-permute-start | bytes 73736 | tf_op jit(solution)/shard_map/ppermute | solution.py:163
Sparse Core Ops, SparseCore 0:
  24.5 15.7 all-gather.5
  41.9 22.5 all-gather.7
  73.9 61.2 all-gather.9
